TPU v7x, 32 devices: a whole 2x2x4 slice. The times are simulated.
32 devices in a mesh: outer: 4 (over y, x), inner: 8 (over z, core).
Axes of the slice: x: 2, y: 2, z: 4, core: 2. Of those that a mesh axis runs over, the one named last changes fastest.
Arguments:
- tokens: bfloat16 [4096, 2048], P(('outer', 'inner')), may hold values from -6 to 6
- cotangent: bfloat16 [4096, 2048], P(('outer', 'inner')), may hold values from -6 to 6
- routes: int32 [4096, 8], P(('outer', 'inner')), may hold values from 0 to 31, all different within a row; in each aligned block of 128 rows (0 to 127, 128 to 255, ...) at most 36 rows name the same one
- router_weight: bfloat16 [2048, 32], replicated, may hold values from -0.125 to 0.125
- gate_saved: bfloat16 [32, 1152, 768], P(('outer', 'inner')), may hold values from -6 to 6
- up_saved: bfloat16 [32, 1152, 768], P(('outer', 'inner')), may hold values from -6 to 6
- gate_weight: bfloat16 [32, 2048, 768], P(('outer', 'inner')), may hold values from -0.125 to 0.125
- up_weight: bfloat16 [32, 2048, 768], P(('outer', 'inner')), may hold values from -0.125 to 0.125
- down_weight: bfloat16 [32, 768, 2048], P(('outer', 'inner')), may hold values from -0.21875 to 0.21875
Outputs:
- grad_tokens: bfloat16 [4096, 2048], P(('outer', 'inner'))
- grad_gate: bfloat16 [32, 2048, 768], P(('outer', 'inner'))
- grad_up: bfloat16 [32, 2048, 768], P(('outer', 'inner'))
- grad_down: bfloat16 [32, 768, 2048], P(('outer', 'inner'))
- grad_router: float32 [2048, 32], replicated
Inputs may be any that keep to these rules, and one draw needn't show every extreme that they name: `routes`: each row names 8 different experts. Among the rows of one device no expert is named more than 36 times, and in every draw some expert is named exactly 36 times by the rows of some device.
All inputs are finite; a program needn't handle non-finite values.
Results may differ from a plain program's by a relative error of at most 0.01.
Values may be sent and summed in bfloat16 or wider, within the bound.
No kernel may reach another device: no remote copies, remote signals or barrier semaphores. Data moves between devices by JAX's collectives and lax.ppermute only.
A program may use at most 192 MiB of HBM per device.

v0:
```python
import math
import jax
import jax.numpy as jnp
from jax import lax
from jax.sharding import PartitionSpec as P

contract_rows = (((0,), (0,)), ((), ()))
contract_cols = (((1,), (1,)), ((), ()))


def route_tables(routes, experts, capacity):
    flat_routes = routes.reshape(-1)
    onehot = (flat_routes[:, None] == jnp.arange(experts, dtype=jnp.int32)[None, :]).astype(
        jnp.int32
    )
    pairs = flat_routes.shape[0]
    lower = (
        jnp.arange(pairs, dtype=jnp.int32)[:, None] > jnp.arange(pairs, dtype=jnp.int32)[None, :]
    ).astype(jnp.bfloat16)
    earlier = jnp.dot(
        lower, onehot.astype(jnp.bfloat16), preferred_element_type=jnp.float32
    ).astype(jnp.int32)
    position = jnp.sum(earlier * onehot, axis=1)
    target = flat_routes * capacity + position
    slot_table = (
        jnp.arange(experts * capacity, dtype=jnp.int32)[:, None] == target[None, :]
    ).astype(jnp.bfloat16)
    token_table = jnp.sum(
        slot_table.reshape(experts * capacity, routes.shape[0], routes.shape[1]), axis=2
    )
    return (slot_table, token_table)


def route_probs(tokens, routes, router_weight):
    router_logits = jnp.dot(tokens, router_weight, preferred_element_type=jnp.float32)
    picked = (
        routes[:, :, None] == jnp.arange(router_weight.shape[1], dtype=jnp.int32)[None, None, :]
    )
    chosen = jnp.sum(jnp.where(picked, router_logits[:, None, :], jnp.float32(0.0)), axis=2)
    exp_terms = jnp.exp(chosen)
    return (picked, exp_terms / jnp.sum(exp_terms, axis=1, keepdims=True))


def dispatch_block(tokens, cotangent, routes, router_weight, capacity):
    picked, probs = route_probs(tokens, routes, router_weight)
    slot_table, token_table = route_tables(routes, router_weight.shape[1], capacity)
    send_tokens = jnp.dot(token_table, tokens, preferred_element_type=jnp.float32).astype(
        jnp.bfloat16
    )
    send_cot = jnp.dot(token_table, cotangent, preferred_element_type=jnp.float32).astype(
        jnp.bfloat16
    )
    probs_low = probs.astype(jnp.bfloat16).reshape(-1)
    send_weight = jnp.dot(slot_table, probs_low, preferred_element_type=jnp.float32).astype(
        jnp.bfloat16
    )
    return (picked, probs, slot_table, token_table, send_tokens, send_cot, send_weight)


def slot_dot(cot_rows, out_rows):
    return jnp.sum(cot_rows.astype(jnp.float32) * out_rows.astype(jnp.float32), axis=1).astype(
        jnp.bfloat16
    )


def expert_backward(
    input_rows, cot_rows, weight_rows, gate_pre, up_pre, gate_matrix, up_matrix, down_matrix
):
    gate_value = gate_pre.astype(jnp.float32)
    up_value = up_pre.astype(jnp.float32)
    sigmoid_gate = jax.nn.sigmoid(gate_value)
    silu_gate = gate_value * sigmoid_gate
    hidden = (silu_gate * up_value).astype(jnp.bfloat16)
    expert_out = jnp.dot(hidden, down_matrix, preferred_element_type=jnp.float32).astype(
        jnp.bfloat16
    )
    scaled_cot = (weight_rows.astype(jnp.float32)[:, None] * cot_rows.astype(jnp.float32)).astype(
        jnp.bfloat16
    )
    grad_hidden = lax.dot_general(
        scaled_cot, down_matrix, contract_cols, preferred_element_type=jnp.float32
    )
    grad_gate_pre = (
        grad_hidden * up_value * sigmoid_gate * (1.0 + gate_value * (1.0 - sigmoid_gate))
    ).astype(jnp.bfloat16)
    grad_up_pre = (grad_hidden * silu_gate).astype(jnp.bfloat16)
    grad_rows = (
        lax.dot_general(
            grad_gate_pre, gate_matrix, contract_cols, preferred_element_type=jnp.float32
        )
        + lax.dot_general(grad_up_pre, up_matrix, contract_cols, preferred_element_type=jnp.float32)
    ).astype(jnp.bfloat16)
    grad_gate_w = lax.dot_general(
        input_rows, grad_gate_pre, contract_rows, preferred_element_type=jnp.float32
    ).astype(jnp.bfloat16)
    grad_up_w = lax.dot_general(
        input_rows, grad_up_pre, contract_rows, preferred_element_type=jnp.float32
    ).astype(jnp.bfloat16)
    grad_down_w = lax.dot_general(
        hidden, scaled_cot, contract_rows, preferred_element_type=jnp.float32
    ).astype(jnp.bfloat16)
    return (grad_rows, expert_out, grad_gate_w, grad_up_w, grad_down_w)


def finish_block(
    tokens, router_weight, picked, probs, slot_table, token_table, back_rows, route_dot
):
    grad_sum = lax.dot_general(
        token_table, back_rows, contract_rows, preferred_element_type=jnp.float32
    )
    route_grad = lax.dot_general(
        slot_table, route_dot, contract_rows, preferred_element_type=jnp.float32
    ).reshape(probs.shape)
    inner_term = jnp.sum(probs * route_grad, axis=1, keepdims=True)
    chosen_grad = probs * (route_grad - inner_term)
    logit_grad = jnp.sum(
        jnp.where(picked, chosen_grad[:, :, None], jnp.float32(0.0)), axis=1
    ).astype(jnp.bfloat16)
    grad_tokens = (
        grad_sum
        + lax.dot_general(
            logit_grad, router_weight, contract_cols, preferred_element_type=jnp.float32
        )
    ).astype(jnp.bfloat16)
    router_part = lax.dot_general(
        tokens, logit_grad, contract_rows, preferred_element_type=jnp.float32
    )
    return (grad_tokens, router_part)


def body(
    tokens,
    cotangent,
    routes,
    router_weight,
    gate_saved,
    up_saved,
    gate_weight,
    up_weight,
    down_weight,
):
    experts = router_weight.shape[1]
    width = tokens.shape[1]
    capacity = gate_saved.shape[1] // experts
    outer_size = lax.axis_size("outer")
    inner_size = lax.axis_size("inner")
    axes = ("outer", "inner")
    picked, probs = route_probs(tokens, routes, router_weight)
    slot_table, token_table = route_tables(routes, experts, capacity)
    both = jnp.concatenate([tokens, cotangent], axis=1)
    grid_both = jnp.dot(
        token_table.reshape(experts, capacity, -1), both, preferred_element_type=jnp.float32
    ).astype(jnp.bfloat16)
    probs_low = probs.astype(jnp.bfloat16).reshape(-1)
    send_weight = jnp.dot(slot_table, probs_low, preferred_element_type=jnp.float32).astype(
        jnp.bfloat16
    )
    grid_weight = send_weight.reshape(experts, capacity)
    got_both = lax.all_to_all(grid_both, axes, split_axis=0, concat_axis=0, tiled=True)
    got_weight = lax.all_to_all(grid_weight, axes, split_axis=0, concat_axis=0, tiled=True)
    got_both = got_both.reshape(-1, 2 * width)
    input_rows = got_both[:, :width]
    cot_rows = got_both[:, width:]
    grad_rows, expert_out, grad_gate_w, grad_up_w, grad_down_w = expert_backward(
        input_rows,
        cot_rows,
        got_weight.reshape(-1),
        gate_saved[0],
        up_saved[0],
        gate_weight[0],
        up_weight[0],
        down_weight[0],
    )
    slot_route_dot = slot_dot(cot_rows, expert_out).reshape(experts, capacity)
    back_dot = lax.all_to_all(slot_route_dot, axes, split_axis=0, concat_axis=0, tiled=True)
    route_dot = back_dot.reshape(-1)
    route_grad = lax.dot_general(
        slot_table, route_dot, contract_rows, preferred_element_type=jnp.float32
    ).reshape(probs.shape)
    inner_term = jnp.sum(probs * route_grad, axis=1, keepdims=True)
    chosen_grad = probs * (route_grad - inner_term)
    logit_grad = jnp.sum(
        jnp.where(picked, chosen_grad[:, :, None], jnp.float32(0.0)), axis=1
    ).astype(jnp.bfloat16)
    router_part = lax.dot_general(
        tokens, logit_grad, contract_rows, preferred_element_type=jnp.float32
    )
    total_tokens = tokens.shape[0] * outer_size * inner_size
    grad_router = lax.psum(router_part, axes) * (1.0 / math.sqrt(total_tokens))
    back_grad = grad_rows.reshape(experts, capacity, width)
    grad_router, back_grad = lax.optimization_barrier((grad_router, back_grad))
    back_rows = lax.all_to_all(back_grad, axes, split_axis=0, concat_axis=0, tiled=True)
    grad_sum = lax.dot_general(
        token_table, back_rows.reshape(-1, width), contract_rows, preferred_element_type=jnp.float32
    )
    grad_tokens = (
        grad_sum
        + lax.dot_general(
            logit_grad, router_weight, contract_cols, preferred_element_type=jnp.float32
        )
    ).astype(jnp.bfloat16)
    return (grad_tokens, grad_gate_w[None], grad_up_w[None], grad_down_w[None], grad_router)


def solution(mesh):
    in_specs = (
        P(("outer", "inner"), None),
        P(("outer", "inner"), None),
        P(("outer", "inner"), None),
        P(),
        P(("outer", "inner"), None, None),
        P(("outer", "inner"), None, None),
        P(("outer", "inner"), None, None),
        P(("outer", "inner"), None, None),
        P(("outer", "inner"), None, None),
    )
    out_specs = (
        P(("outer", "inner"), None),
        P(("outer", "inner"), None, None),
        P(("outer", "inner"), None, None),
        P(("outer", "inner"), None, None),
        P(),
    )
    return jax.shard_map(body, mesh=mesh, in_specs=in_specs, out_specs=out_specs, check_vma=False)
```

profile of v0, /device:TPU:0, one launch (start us, length us, event | category | flops | bytes accessed | tf_op | source)
XLA Modules:
  0.0 579.3 jit_solution(17009639620150459499)
XLA Ops:
  9.6 6.0 %fusion.51 = bf16[1152,128]{1,0:T(8,128)(2,1)S(1)} fusion(s32[128,8]{0,1:T(8,128)S(1)} %multiply_add_fusion.1), kind=kLoop, calls=%fused_computation.57 | loop fusion | flops 3391488 | bytes 299008 | tf_op jit(solution)/shard_map/reduce_sum | solution.py:28
  16.4 8.0 %convolution_convert_fusion = bf16[32,36,4096]{2,1,0:T(8,128)(2,1)} fusion(bf16[32,36,128]{2,1,0:T(8,128)(2,1)} %reshape.116, bf16[128,2048]{1,0:T(8,128)(2,1)} %param.10, bf16[128,2048]{1,0:T(8,128)(2,1)} %param.9), kind=kOutput, calls=%fused_computation.5 | convolution fusion | flops 1214775296 | bytes 10780672 | tf_op jit(solution)/shard_map/dot_general | solution.py:151
  24.4 7.4 %all-to-all-start = ((bf16[32,36,4096]{2,1,0:T(8,128)(2,1)}), bf16[32,36,4096]{2,1,0:T(8,128)(2,1)}, u32[]{:S(2)}, u32[]{:S(2)}) async-start(bf16[32,36,4096]{2,1,0:T(8,128)(2,1)} %convolution_convert_fusion), calls=%async_computation | async-start | bytes 20971520 | tf_op jit(solution)/shard_map/all_to_all | solution.py:159
  33.3 228.5 %all-to-all-done = bf16[32,36,4096]{2,1,0:T(8,128)(2,1)} async-done(((bf16[32,36,4096]{2,1,0:T(8,128)(2,1)}), bf16[32,36,4096]{2,1,0:T(8,128)(2,1)}, u32[]{:S(2)}, u32[]{:S(2)}) %all-to-all-start) | async-done | bytes 9437216 | tf_op jit(solution)/shard_map/all_to_all | solution.py:159
  261.7 13.2 %reshape.117 = bf16[1152,4096]{1,0:T(8,128)(2,1)} reshape(bf16[32,36,4096]{2,1,0:T(8,128)(2,1)} %all-to-all-done) | data formatting | bytes 18874368 | tf_op jit(solution)/shard_map/reshape | solution.py:161
  274.9 8.6 %fusion = bf16[1152]{0:T(1024)(128)(2,1)S(1)} fusion(bf16[1152,4096]{1,0:T(8,128)(2,1)} %reshape.117, bf16[1,768,2048]{2,1,0:T(8,128)(2,1)} %param.17, bf16[1,1152,768]{2,1,0:T(8,128)(2,1)} %param.14, bf16[1,1152,768]{2,1,0:T(8,128)(2,1)} %param.13), kind=kOutput, calls=%fused_computation.2 | convolution fusion | flops 3642752000 | bytes 11405568 | tf_op jit(solution)/shard_map/dot_general | solution.py:74
  284.3 2.7 all-to-all-start.1
  287.1 6.9 %all-to-all-done.1 = bf16[32,1,36]{2,1,0:T(2,128)(2,1)S(1)} async-done(((bf16[32,1,36]{2,1,0:T(2,128)(2,1)}), bf16[32,1,36]{2,1,0:T(2,128)(2,1)S(1)}, u32[]{:S(2)}, u32[]{:S(2)}) %all-to-all-start.1) | async-done | bytes 2336 | tf_op jit(solution)/shard_map/all_to_all | solution.py:175
  294.1 5.9 %fusion.8 = f32[1,128,8]{2,0,1:T(1,128)S(1)} fusion(bf16[1152,1,1]{0,1,2:T(2,128)(2,1)S(1)} %reshape.125, s32[1024]{0:T(1024)S(1)} %multiply_add_fusion), kind=kOutput, calls=%fused_computation.19 | convolution fusion | flops 3538944 | bytes 10496 | tf_op jit(solution)/shard_map/dot_general | solution.py:177
  302.0 2.5 all-to-all-start.2
  304.6 2.0 convolution_bitcast_fusion
  306.6 5.0 all-to-all-done.2
  311.8 9.1 %fusion.19 = (bf16[1152,768]{1,0:T(8,128)(2,1)S(1)}, f32[1152,768]{1,0:T(8,128)S(1)}) fusion(bf16[1,1152,768]{2,1,0:T(8,128)(2,1)} %param.14, bf16[1,1152,768]{2,1,0:T(8,128)(2,1)} %param.13, bf16[1,768,2048]{2,1,0:T(8,128)(2,1)} %param.17, f32[1152]{0:T(1024)S(1)} %reshape.121, bf16[1152,4096]{1,0:T(8,128)(2,1)} %reshape.117), kind=kOutput, calls=%fused_computation.32 | convolution fusion | flops 3641573376 | bytes 16716288 | tf_op jit(solution)/shard_map/dot_general | solution.py:80
  321.0 6.3 %fusion.36 = f32[1152,2048]{1,0:T(8,128)} fusion(bf16[1152,768]{1,0:T(8,128)(2,1)S(1)} %get-tuple-element.11, bf16[1,2048,768]{2,1,0:T(8,128)(2,1)S(1)} %copy-done), kind=kOutput, calls=%fused_computation.47 | convolution fusion | flops 3623878656 | bytes 14352384 | tf_op jit(solution)/shard_map/dot_general | solution.py:88
  327.4 8.4 %add_convert_fusion = bf16[1152,2048]{1,0:T(8,128)(2,1)} fusion(f32[1152,2048]{1,0:T(8,128)} %fusion.36, bf16[1,2048,768]{2,1,0:T(8,128)(2,1)S(1)} %copy-done.4, f32[1152,768]{1,0:T(8,128)S(1)} %get-tuple-element.12, bf16[1,1152,768]{2,1,0:T(8,128)(2,1)S(1)} %copy-done.6), kind=kOutput, calls=%fused_computation.4 | convolution fusion | flops 3634790400 | bytes 22609920 | tf_op jit(solution)/shard_map/dot_general | solution.py:91
  335.8 7.2 %reshape.119 = bf16[32,36,2048]{2,1,0:T(8,128)(2,1)} reshape(bf16[1152,2048]{1,0:T(8,128)(2,1)} %add_convert_fusion) | data formatting | bytes 9437184 | tf_op jit(solution)/shard_map/reshape | solution.py:190
  343.0 94.8 %all-reduce.2.cloned.1.call-done = f32[2048,32]{0,1:T(8,128)} async-done(((f32[2048,32]{0,1:T(8,128)}), f32[2048,32]{0,1:T(8,128)}) %all-reduce.2.cloned.1.call-update) | async-done | bytes 262160 | tf_op jit(solution)/shard_map/psum | solution.py:189
  439.4 4.0 all-to-all-start.3
  443.4 9.1 %fusion.45 = bf16[1,2048,768]{2,1,0:T(8,128)(2,1)} fusion(bf16[1152,768]{1,0:T(8,128)(2,1)} %copy-done.10, bf16[1152,4096]{1,0:T(8,128)(2,1)} %reshape.117), kind=kOutput, calls=%fused_computation.54 | convolution fusion | flops 3625451520 | bytes 9633792 | tf_op jit(solution)/shard_map/dot_general | solution.py:93
  452.5 9.1 %fusion.41 = bf16[1,768,2048]{2,1,0:T(8,128)(2,1)} fusion(bf16[1,1152,768]{2,1,0:T(8,128)(2,1)S(1)} %copy-done.5, bf16[1,1152,768]{2,1,0:T(8,128)(2,1)S(1)} %copy-done.7, f32[1152]{0:T(1024)S(1)} %reshape.121, bf16[1152,4096]{1,0:T(8,128)(2,1)} %reshape.117), kind=kOutput, calls=%fused_computation.52 | convolution fusion | flops 3639607296 | bytes 11407872 | tf_op jit(solution)/shard_map/dot_general | solution.py:99
  461.7 6.3 %fusion.42 = bf16[1,2048,768]{2,1,0:T(8,128)(2,1)} fusion(bf16[1152,4096]{1,0:T(8,128)(2,1)S(1)} %bitcast.97, f32[1152,768]{1,0:T(8,128)S(1)} %copy-done.9, bf16[1,1152,768]{2,1,0:T(8,128)(2,1)S(1)} %copy-done.7), kind=kOutput, calls=%fused_computation.53 | convolution fusion | flops 3631644672 | bytes 13172736 | tf_op jit(solution)/shard_map/dot_general | solution.py:96
  468.0 92.7 %all-to-all-done.3 = bf16[32,36,2048]{2,1,0:T(8,128)(2,1)} async-done(((bf16[32,36,2048]{2,1,0:T(8,128)(2,1)}), bf16[32,36,2048]{2,1,0:T(8,128)(2,1)}, u32[]{:S(2)}, u32[]{:S(2)}) %all-to-all-start.3) | async-done | bytes 4718624 | tf_op jit(solution)/shard_map/all_to_all | solution.py:192
  560.7 7.4 %reshape.120 = bf16[1152,2048]{1,0:T(8,128)(2,1)} reshape(bf16[32,36,2048]{2,1,0:T(8,128)(2,1)} %all-to-all-done.3) | data formatting | bytes 9437184 | tf_op jit(solution)/shard_map/reshape | solution.py:194
  568.1 3.2 fusion.76
  (57 shorter events, 10.6 us)
Async XLA Ops:
  7.2 313.8 %copy-start = (bf16[1,2048,768]{2,1,0:T(8,128)(2,1)S(1)}, bf16[1,2048,768]{2,1,0:T(8,128)(2,1)}, u32[]{:S(2)}) copy-start(bf16[1,2048,768]{2,1,0:T(8,128)(2,1)} %param.15) | copy-start | bytes 9437188
  24.4 8.8 %copy-start.3 = (s32[128,8]{0,1:T(8,128)S(1)}, s32[128,8]{0,1:T(8,128)}, u32[]{:S(2)}) copy-start(s32[128,8]{0,1:T(8,128)} %param.11) | copy-start | bytes 12292
  24.4 237.3 %all-to-all-start = ((bf16[32,36,4096]{2,1,0:T(8,128)(2,1)}), bf16[32,36,4096]{2,1,0:T(8,128)(2,1)}, u32[]{:S(2)}, u32[]{:S(2)}) async-start(bf16[32,36,4096]{2,1,0:T(8,128)(2,1)} %convolution_convert_fusion), calls=%async_computation | async-start | bytes 20971520 | tf_op jit(solution)/shard_map/all_to_all | solution.py:159
  284.3 9.6 %all-to-all-start.1 = ((bf16[32,1,36]{2,1,0:T(2,128)(2,1)}), bf16[32,1,36]{2,1,0:T(2,128)(2,1)S(1)}, u32[]{:S(2)}, u32[]{:S(2)}) async-start(bf16[32,1,36]{2,1,0:T(2,128)(2,1)} %convert_element_type.152), calls=%async_computation.1 | async-start | bytes 32768 | tf_op jit(solution)/shard_map/all_to_all | solution.py:175
  302.0 9.6 %all-to-all-start.2 = ((bf16[32,1,36]{2,1,0:T(2,128)(2,1)}), bf16[32,1,36]{2,1,0:T(2,128)(2,1)S(1)}, u32[]{:S(2)}, u32[]{:S(2)}) async-start(bf16[32,1,36]{2,1,0:T(2,128)(2,1)} %all_to_all.21), calls=%async_computation.2 | async-start | bytes 32768 | tf_op jit(solution)/shard_map/all_to_all | solution.py:160
  304.6 133.2 %all-reduce.2.cloned.1.call-start = ((), (), s32[]{:S(2)}) async-start(), calls=%async_computation.4 | async-start | bytes 524288 | tf_op jit(solution)/shard_map/psum | solution.py:189
  320.9 6.3 %copy-start.10 = (bf16[1152,768]{1,0:T(8,128)(2,1)}, bf16[1152,768]{1,0:T(8,128)(2,1)S(1)}, u32[]{:S(2)}) copy-start(bf16[1152,768]{1,0:T(8,128)(2,1)S(1)} %get-tuple-element.11) | copy-start | bytes 5308420
  320.9 6.4 %copy-start.8 = (f32[1152,768]{1,0:T(8,128)}, f32[1152,768]{1,0:T(8,128)S(1)}, u32[]{:S(2)}) copy-start(f32[1152,768]{1,0:T(8,128)S(1)} %get-tuple-element.12) | copy-start | bytes 10616836
  321.0 6.4 %copy-start.4 = (bf16[1,2048,768]{2,1,0:T(8,128)(2,1)S(1)}, bf16[1,2048,768]{2,1,0:T(8,128)(2,1)}, u32[]{:S(2)}) copy-start(bf16[1,2048,768]{2,1,0:T(8,128)(2,1)} %param.16) | copy-start | bytes 9437188
  321.0 6.4 %copy-start.6 = (bf16[1,1152,768]{2,1,0:T(8,128)(2,1)S(1)}, bf16[1,1152,768]{2,1,0:T(8,128)(2,1)}, u32[]{:S(2)}) copy-start(bf16[1,1152,768]{2,1,0:T(8,128)(2,1)} %param.13) | copy-start | bytes 5308420
  439.4 121.3 %all-to-all-start.3 = ((bf16[32,36,2048]{2,1,0:T(8,128)(2,1)}), bf16[32,36,2048]{2,1,0:T(8,128)(2,1)}, u32[]{:S(2)}, u32[]{:S(2)}) async-start(bf16[32,36,2048]{2,1,0:T(8,128)(2,1)} %reshape.119), calls=%async_computation.3 | async-start | bytes 10485760 | tf_op jit(solution)/shard_map/all_to_all | solution.py:192
  443.4 9.1 %copy-start.5 = (bf16[1,1152,768]{2,1,0:T(8,128)(2,1)S(1)}, bf16[1,1152,768]{2,1,0:T(8,128)(2,1)}, u32[]{:S(2)}) copy-start(bf16[1,1152,768]{2,1,0:T(8,128)(2,1)} %param.14) | copy-start | bytes 5308420
  443.4 9.1 %copy-start.7 = (bf16[1,1152,768]{2,1,0:T(8,128)(2,1)S(1)}, bf16[1,1152,768]{2,1,0:T(8,128)(2,1)}, u32[]{:S(2)}) copy-start(bf16[1,1152,768]{2,1,0:T(8,128)(2,1)} %param.13) | copy-start | bytes 5308420
  443.4 18.2 %slice-start = ((s8[9437184]{0:T(1024)(128)(4,1)}), s8[4194304]{0:T(1024)(128)(4,1)S(1)}, s32[]{:S(2)}) async-start(s8[9437184]{0:T(1024)(128)(4,1)} %bitcast.96), calls=%async_computation.5 | async-start | bytes 8388608
  443.4 18.2 %slice-start.1 = ((s8[9437184]{0:T(1024)(128)(4,1)}), s8[4194304]{0:T(1024)(128)(4,1)S(1)}, s32[]{:S(2)}) async-start(s8[9437184]{0:T(1024)(128)(4,1)} %bitcast.96), calls=%async_computation.6 | async-start | bytes 8388608
  452.5 9.1 %slice-start.2 = ((s8[9437184]{0:T(1024)(128)(4,1)}), s8[1048576]{0:T(1024)(128)(4,1)S(1)}, s32[]{:S(2)}) async-start(s8[9437184]{0:T(1024)(128)(4,1)} %bitcast.96), calls=%async_computation.7 | async-start | bytes 2097152
  452.5 9.1 %copy-start.9 = (f32[1152,768]{1,0:T(8,128)S(1)}, f32[1152,768]{1,0:T(8,128)}, u32[]{:S(2)}) copy-start(f32[1152,768]{1,0:T(8,128)} %copy-done.8) | copy-start | bytes 10616836
  560.7 11.8 %copy-start.1 = (bf16[1,2048,768]{2,1,0:T(8,128)(2,1)S(1)}, bf16[1,2048,768]{2,1,0:T(8,128)(2,1)}, u32[]{:S(2)}) copy-start(bf16[1,2048,768]{2,1,0:T(8,128)(2,1)} %param.15) | copy-start | bytes 9437188
  568.1 3.3 copy-start.2
Sparse Core Ops, SparseCore 0:
  311.5 126.2 all-reduce.1
where the time goes:
time: 580 us; the launch traced here: 579 us
  waiting for transfers between devices  428 us (74%)
  matrix products  79.9 us (14%)
  local copies, waits for them, and re-layouts  31.9 us (6%)
  starting transfers between devices  16.7 us (3%)
  between operations  14.3 us (2%)
  other arithmetic  8.64 us (1%)
    all_to_all x1, waiting for transfers between devices, body(): lax.all_to_all(grid_both, axes, split_axis=0, concat_axis=0, tiled=True)  228 us
    psum x1, waiting for transfers between devices, body(): grad_router = lax.psum(router_part, axes) * (1.0 / math.sqrt(total_tokens))  94.8 us
    all_to_all x1, waiting for transfers between devices, body(): lax.all_to_all(back_grad, axes, split_axis=0, concat_axis=0, tiled=True)  92.7 us
    reshape x1, local copies, waits for them, and re-layouts, body(): got_both = got_both.reshape(-1, 2 * width)  13.2 us
  transfers between devices with their start and end apart: 5, of which 5 were waited for; matrix products, arithmetic and copies ran while one was open for 10% of the time, Pallas kernels for 0%

commit v1 on v0

--- a/solution.py
+++ b/solution.py
@@ -186,7 +186,9 @@
         tokens, logit_grad, contract_rows, preferred_element_type=jnp.float32
     )
     total_tokens = tokens.shape[0] * outer_size * inner_size
-    grad_router = lax.psum(router_part, axes) * (1.0 / math.sqrt(total_tokens))
+    grad_router = jnp.sum(lax.all_gather(router_part, axes), axis=0) * (
+        1.0 / math.sqrt(total_tokens)
+    )
     back_grad = grad_rows.reshape(experts, capacity, width)
     grad_router, back_grad = lax.optimization_barrier((grad_router, back_grad))
     back_rows = lax.all_to_all(back_grad, axes, split_axis=0, concat_axis=0, tiled=True)

time: 580 us -> 535 us (0.922); the launches traced: 579 us -> 527 us
  waiting for transfers between devices: 428 us -> 360 us
  blocking collectives: 0 us -> 8.85 us
  local copies, waits for them, and re-layouts: 31.9 us -> 39.8 us
    psum x1 -> x0, waiting for transfers between devices: 94.8 us -> none  [body(): grad_router = lax.psum(router_part, axes) * (1.0 / math.sqrt(total_tokens))]
    all_gather x0 -> x1, waiting for transfers between devices: none -> 32.4 us  [body(): lax.all_gather(router_part, axes)]
    all_to_all x0 -> x1, blocking collectives: none -> 8.85 us  [body(): lax.all_to_all(grid_weight, axes, split_axis=0, concat_axis=0, tiled=True)]
    unnamed x29 -> x30, local copies, waits for them, and re-layouts: 1.12 us -> 9.44 us
  transfers between devices with their start and end apart: 5 -> 4, of which waited for: 5 -> 4; matrix products, arithmetic and copies ran while one was open for 10% -> 11% of each run, Pallas kernels for 0% -> 0%
where the time goes in v1:
time: 535 us; the launch traced here: 527 us
  waiting for transfers between devices  360 us (67%)
  matrix products  79.9 us (15%)
  local copies, waits for them, and re-layouts  39.8 us (7%)
  between operations  14.5 us (3%)
  starting transfers between devices  14.3 us (3%)
  other arithmetic  8.99 us (2%)
  blocking collectives  8.85 us (2%)
    all_to_all x1, waiting for transfers between devices, body(): lax.all_to_all(grid_both, axes, split_axis=0, concat_axis=0, tiled=True)  228 us
    all_to_all x1, waiting for transfers between devices, body(): lax.all_to_all(back_grad, axes, split_axis=0, concat_axis=0, tiled=True)  92.9 us
    all_gather x1, waiting for transfers between devices, body(): lax.all_gather(router_part, axes)  32.4 us
    reshape x1, local copies, waits for them, and re-layouts, body(): got_both = got_both.reshape(-1, 2 * width)  13.2 us
  transfers between devices with their start and end apart: 4, of which 4 were waited for; matrix products, arithmetic and copies ran while one was open for 11% of the time, Pallas kernels for 0%

profile of v1, /device:TPU:0, one launch (start us, length us, event | category | flops | bytes accessed | tf_op | source)
XLA Modules:
  0.0 526.6 jit_solution(7940125675408145011)
XLA Ops:
  9.6 6.0 %fusion.51 = bf16[1152,128]{1,0:T(8,128)(2,1)S(1)} fusion(s32[128,8]{0,1:T(8,128)S(1)} %multiply_add_fusion.1), kind=kLoop, calls=%fused_computation.58 | loop fusion | flops 3391488 | bytes 299008 | tf_op jit(solution)/shard_map/reduce_sum | solution.py:28
  16.4 8.0 %convolution_convert_fusion = bf16[32,36,4096]{2,1,0:T(8,128)(2,1)} fusion(bf16[32,36,128]{2,1,0:T(8,128)(2,1)} %reshape.116, bf16[128,2048]{1,0:T(8,128)(2,1)} %param.10, bf16[128,2048]{1,0:T(8,128)(2,1)} %param.9), kind=kOutput, calls=%fused_computation.6 | convolution fusion | flops 1214775296 | bytes 10780672 | tf_op jit(solution)/shard_map/dot_general | solution.py:151
  24.4 7.4 %all-to-all-start = ((bf16[32,36,4096]{2,1,0:T(8,128)(2,1)}), bf16[32,36,4096]{2,1,0:T(8,128)(2,1)}, u32[]{:S(2)}, u32[]{:S(2)}) async-start(bf16[32,36,4096]{2,1,0:T(8,128)(2,1)} %convolution_convert_fusion), calls=%async_computation | async-start | bytes 20971520 | tf_op jit(solution)/shard_map/all_to_all | solution.py:159
  33.3 228.5 %all-to-all-done = bf16[32,36,4096]{2,1,0:T(8,128)(2,1)} async-done(((bf16[32,36,4096]{2,1,0:T(8,128)(2,1)}), bf16[32,36,4096]{2,1,0:T(8,128)(2,1)}, u32[]{:S(2)}, u32[]{:S(2)}) %all-to-all-start) | async-done | bytes 9437216 | tf_op jit(solution)/shard_map/all_to_all | solution.py:159
  261.7 13.2 %reshape.117 = bf16[1152,4096]{1,0:T(8,128)(2,1)} reshape(bf16[32,36,4096]{2,1,0:T(8,128)(2,1)} %all-to-all-done) | data formatting | bytes 18874368 | tf_op jit(solution)/shard_map/reshape | solution.py:161
  274.9 8.6 %fusion = bf16[1152]{0:T(1024)(128)(2,1)S(1)} fusion(bf16[1152,4096]{1,0:T(8,128)(2,1)} %reshape.117, bf16[1,768,2048]{2,1,0:T(8,128)(2,1)} %param.17, bf16[1,1152,768]{2,1,0:T(8,128)(2,1)} %param.14, bf16[1,1152,768]{2,1,0:T(8,128)(2,1)} %param.13), kind=kOutput, calls=%fused_computation.2 | convolution fusion | flops 3642752000 | bytes 11405568 | tf_op jit(solution)/shard_map/dot_general | solution.py:74
  284.3 2.5 all-to-all-start.1
  287.4 6.5 %all-to-all-done.1 = bf16[32,1,36]{2,1,0:T(2,128)(2,1)S(1)} async-done(((bf16[32,1,36]{2,1,0:T(2,128)(2,1)}), bf16[32,1,36]{2,1,0:T(2,128)(2,1)S(1)}, u32[]{:S(2)}, u32[]{:S(2)}) %all-to-all-start.1) | async-done | bytes 2336 | tf_op jit(solution)/shard_map/all_to_all | solution.py:175
  294.1 5.9 %fusion.8 = f32[1,128,8]{2,0,1:T(1,128)S(1)} fusion(bf16[1152,1,1]{0,1,2:T(2,128)(2,1)S(1)} %reshape.126, s32[1024]{0:T(1024)S(1)} %multiply_add_fusion), kind=kOutput, calls=%fused_computation.20 | convolution fusion | flops 3538944 | bytes 10496 | tf_op jit(solution)/shard_map/dot_general | solution.py:177
  300.2 2.0 convolution_bitcast_fusion
  303.4 8.8 %all_to_all.26 = bf16[32,1,36]{2,1,0:T(2,128)(2,1)S(1)} all-to-all(bf16[32,1,36]{2,1,0:T(2,128)(2,1)S(1)} %all_to_all.21), channel_id=1, replica_groups=mesh['outer'=4,'inner'=8] {'outer','inner'}, dimensions={0} | all-to-all | bytes 4608 | tf_op jit(solution)/shard_map/all_to_all | solution.py:160
  312.4 9.2 %fusion.19 = (bf16[1152,768]{1,0:T(8,128)(2,1)S(1)}, f32[1152,768]{1,0:T(8,128)S(1)}) fusion(bf16[1,1152,768]{2,1,0:T(8,128)(2,1)} %param.14, bf16[1,1152,768]{2,1,0:T(8,128)(2,1)} %param.13, bf16[1,768,2048]{2,1,0:T(8,128)(2,1)} %param.17, f32[1152]{0:T(1024)S(1)} %reshape.121, bf16[1152,4096]{1,0:T(8,128)(2,1)} %reshape.117), kind=kOutput, calls=%fused_computation.33 | convolution fusion | flops 3641573376 | bytes 16716288 | tf_op jit(solution)/shard_map/dot_general | solution.py:80
  321.6 6.3 %fusion.36 = f32[1152,2048]{1,0:T(8,128)} fusion(bf16[1152,768]{1,0:T(8,128)(2,1)S(1)} %get-tuple-element.11, bf16[1,2048,768]{2,1,0:T(8,128)(2,1)S(1)} %copy-done), kind=kOutput, calls=%fused_computation.48 | convolution fusion | flops 3623878656 | bytes 14352384 | tf_op jit(solution)/shard_map/dot_general | solution.py:88
  328.0 8.3 %add_convert_fusion = bf16[1152,2048]{1,0:T(8,128)(2,1)} fusion(f32[1152,2048]{1,0:T(8,128)} %fusion.36, bf16[1,2048,768]{2,1,0:T(8,128)(2,1)S(1)} %copy-done.4, f32[1152,768]{1,0:T(8,128)S(1)} %get-tuple-element.12, bf16[1,1152,768]{2,1,0:T(8,128)(2,1)S(1)} %copy-done.6), kind=kOutput, calls=%fused_computation.4 | convolution fusion | flops 3634790400 | bytes 22609920 | tf_op jit(solution)/shard_map/dot_general | solution.py:91
  336.3 7.4 %reshape.119 = bf16[32,36,2048]{2,1,0:T(8,128)(2,1)} reshape(bf16[1152,2048]{1,0:T(8,128)(2,1)} %add_convert_fusion) | data formatting | bytes 9437184 | tf_op jit(solution)/shard_map/reshape | solution.py:192
  343.7 32.4 %all-gather.3.cloned.1.call-done = f32[65536,32]{0,1:T(8,128)} async-done(((f32[2048,32]{0,1:T(8,128)}), f32[65536,32]{0,1:T(8,128)}) %all-gather.3.cloned.1.call-update) | async-done | bytes 8388624 | tf_op jit(solution)/shard_map/all_gather | solution.py:189
  376.1 8.3 %copy.42 = f32[4,8,32,2048]{3,2,1,0:T(8,128)S(1)} copy(f32[4,8,32,2048]{3,1,2,0:T(8,128)} %bitcast.103) | data formatting | bytes 16777216
  386.4 3.8 all-to-all-start.3
  390.3 9.1 %fusion.45 = bf16[1,2048,768]{2,1,0:T(8,128)(2,1)} fusion(bf16[1152,768]{1,0:T(8,128)(2,1)} %copy-done.10, bf16[1152,4096]{1,0:T(8,128)(2,1)} %reshape.117), kind=kOutput, calls=%fused_computation.55 | convolution fusion | flops 3625451520 | bytes 9633792 | tf_op jit(solution)/shard_map/dot_general | solution.py:93
  399.4 9.1 %fusion.41 = bf16[1,768,2048]{2,1,0:T(8,128)(2,1)} fusion(bf16[1,1152,768]{2,1,0:T(8,128)(2,1)S(1)} %copy-done.5, bf16[1,1152,768]{2,1,0:T(8,128)(2,1)S(1)} %copy-done.7, f32[1152]{0:T(1024)S(1)} %reshape.121, bf16[1152,4096]{1,0:T(8,128)(2,1)} %reshape.117), kind=kOutput, calls=%fused_computation.53 | convolution fusion | flops 3639607296 | bytes 11407872 | tf_op jit(solution)/shard_map/dot_general | solution.py:99
  408.5 6.3 %fusion.42 = bf16[1,2048,768]{2,1,0:T(8,128)(2,1)} fusion(bf16[1152,4096]{1,0:T(8,128)(2,1)S(1)} %bitcast.102, f32[1152,768]{1,0:T(8,128)S(1)} %copy-done.9, bf16[1,1152,768]{2,1,0:T(8,128)(2,1)S(1)} %copy-done.7), kind=kOutput, calls=%fused_computation.54 | convolution fusion | flops 3631644672 | bytes 13172736 | tf_op jit(solution)/shard_map/dot_general | solution.py:96
  414.8 92.9 %all-to-all-done.3 = bf16[32,36,2048]{2,1,0:T(8,128)(2,1)} async-done(((bf16[32,36,2048]{2,1,0:T(8,128)(2,1)}), bf16[32,36,2048]{2,1,0:T(8,128)(2,1)}, u32[]{:S(2)}, u32[]{:S(2)}) %all-to-all-start.3) | async-done | bytes 4718624 | tf_op jit(solution)/shard_map/all_to_all | solution.py:194
  507.7 7.4 %reshape.120 = bf16[1152,2048]{1,0:T(8,128)(2,1)} reshape(bf16[32,36,2048]{2,1,0:T(8,128)(2,1)} %all-to-all-done.3) | data formatting | bytes 9437184 | tf_op jit(solution)/shard_map/reshape | solution.py:196
  515.1 3.2 fusion.76
  (58 shorter events, 10.9 us)
Async XLA Ops:
  7.2 314.4 %copy-start = (bf16[1,2048,768]{2,1,0:T(8,128)(2,1)S(1)}, bf16[1,2048,768]{2,1,0:T(8,128)(2,1)}, u32[]{:S(2)}) copy-start(bf16[1,2048,768]{2,1,0:T(8,128)(2,1)} %param.15) | copy-start | bytes 9437188
  24.4 8.8 %copy-start.3 = (s32[128,8]{0,1:T(8,128)S(1)}, s32[128,8]{0,1:T(8,128)}, u32[]{:S(2)}) copy-start(s32[128,8]{0,1:T(8,128)} %param.11) | copy-start | bytes 12292
  24.4 237.3 %all-to-all-start = ((bf16[32,36,4096]{2,1,0:T(8,128)(2,1)}), bf16[32,36,4096]{2,1,0:T(8,128)(2,1)}, u32[]{:S(2)}, u32[]{:S(2)}) async-start(bf16[32,36,4096]{2,1,0:T(8,128)(2,1)} %convolution_convert_fusion), calls=%async_computation | async-start | bytes 20971520 | tf_op jit(solution)/shard_map/all_to_all | solution.py:159
  284.3 9.6 %all-to-all-start.1 = ((bf16[32,1,36]{2,1,0:T(2,128)(2,1)}), bf16[32,1,36]{2,1,0:T(2,128)(2,1)S(1)}, u32[]{:S(2)}, u32[]{:S(2)}) async-start(bf16[32,1,36]{2,1,0:T(2,128)(2,1)} %convert_element_type.152), calls=%async_computation.1 | async-start | bytes 32768 | tf_op jit(solution)/shard_map/all_to_all | solution.py:175
  286.9 89.2 %all-gather.3.cloned.1.call-start = ((), (), s32[]{:S(2)}) async-start(), calls=%async_computation.4 | async-start | bytes 8650752 | tf_op jit(solution)/shard_map/all_gather | solution.py:189
  321.6 6.3 %copy-start.10 = (bf16[1152,768]{1,0:T(8,128)(2,1)}, bf16[1152,768]{1,0:T(8,128)(2,1)S(1)}, u32[]{:S(2)}) copy-start(bf16[1152,768]{1,0:T(8,128)(2,1)S(1)} %get-tuple-element.11) | copy-start | bytes 5308420
  321.6 6.4 %copy-start.8 = (f32[1152,768]{1,0:T(8,128)}, f32[1152,768]{1,0:T(8,128)S(1)}, u32[]{:S(2)}) copy-start(f32[1152,768]{1,0:T(8,128)S(1)} %get-tuple-element.12) | copy-start | bytes 10616836
  321.6 6.4 %copy-start.4 = (bf16[1,2048,768]{2,1,0:T(8,128)(2,1)S(1)}, bf16[1,2048,768]{2,1,0:T(8,128)(2,1)}, u32[]{:S(2)}) copy-start(bf16[1,2048,768]{2,1,0:T(8,128)(2,1)} %param.16) | copy-start | bytes 9437188
  321.6 6.4 %copy-start.6 = (bf16[1,1152,768]{2,1,0:T(8,128)(2,1)S(1)}, bf16[1,1152,768]{2,1,0:T(8,128)(2,1)}, u32[]{:S(2)}) copy-start(bf16[1,1152,768]{2,1,0:T(8,128)(2,1)} %param.13) | copy-start | bytes 5308420
  386.4 121.3 %all-to-all-start.3 = ((bf16[32,36,2048]{2,1,0:T(8,128)(2,1)}), bf16[32,36,2048]{2,1,0:T(8,128)(2,1)}, u32[]{:S(2)}, u32[]{:S(2)}) async-start(bf16[32,36,2048]{2,1,0:T(8,128)(2,1)} %reshape.119), calls=%async_computation.3 | async-start | bytes 10485760 | tf_op jit(solution)/shard_map/all_to_all | solution.py:194
  390.2 9.1 %copy-start.5 = (bf16[1,1152,768]{2,1,0:T(8,128)(2,1)S(1)}, bf16[1,1152,768]{2,1,0:T(8,128)(2,1)}, u32[]{:S(2)}) copy-start(bf16[1,1152,768]{2,1,0:T(8,128)(2,1)} %param.14) | copy-start | bytes 5308420
  390.2 9.1 %copy-start.7 = (bf16[1,1152,768]{2,1,0:T(8,128)(2,1)S(1)}, bf16[1,1152,768]{2,1,0:T(8,128)(2,1)}, u32[]{:S(2)}) copy-start(bf16[1,1152,768]{2,1,0:T(8,128)(2,1)} %param.13) | copy-start | bytes 5308420
  390.3 18.2 %slice-start = ((s8[9437184]{0:T(1024)(128)(4,1)}), s8[4194304]{0:T(1024)(128)(4,1)S(1)}, s32[]{:S(2)}) async-start(s8[9437184]{0:T(1024)(128)(4,1)} %bitcast.101), calls=%async_computation.5 | async-start | bytes 8388608
  390.3 18.2 %slice-start.1 = ((s8[9437184]{0:T(1024)(128)(4,1)}), s8[4194304]{0:T(1024)(128)(4,1)S(1)}, s32[]{:S(2)}) async-start(s8[9437184]{0:T(1024)(128)(4,1)} %bitcast.101), calls=%async_computation.6 | async-start | bytes 8388608
  399.3 9.1 %slice-start.2 = ((s8[9437184]{0:T(1024)(128)(4,1)}), s8[1048576]{0:T(1024)(128)(4,1)S(1)}, s32[]{:S(2)}) async-start(s8[9437184]{0:T(1024)(128)(4,1)} %bitcast.101), calls=%async_computation.7 | async-start | bytes 2097152
  399.3 9.1 %copy-start.9 = (f32[1152,768]{1,0:T(8,128)S(1)}, f32[1152,768]{1,0:T(8,128)}, u32[]{:S(2)}) copy-start(f32[1152,768]{1,0:T(8,128)} %copy-done.8) | copy-start | bytes 10616836
  507.7 11.8 %copy-start.1 = (bf16[1,2048,768]{2,1,0:T(8,128)(2,1)S(1)}, bf16[1,2048,768]{2,1,0:T(8,128)(2,1)}, u32[]{:S(2)}) copy-start(bf16[1,2048,768]{2,1,0:T(8,128)(2,1)} %param.15) | copy-start | bytes 9437188
  515.1 3.3 copy-start.2
Sparse Core Ops, SparseCore 0:
  302.3 73.7 all-gather.2
